TPU v7x, 32 devices: a whole 2x2x4 slice. The times are simulated.
32 devices in a mesh: dp: 8 (over z, core), shard: 4 (over y, x).
Axes of the slice: x: 2, y: 2, z: 4, core: 2. Of those that a mesh axis runs over, the one named last changes fastest.
Arguments:
- grad_partials: bfloat16 [8, 32, 256, 256], P('dp', 'shard'), may hold values from -8 to 8
- owners: int32 [32, 1], P('shard'), may hold values from 0 to 7; in each aligned block of 8 rows (0 to 7, 8 to 15, ...) at most 2 rows name the same one
- weight_blocks: int32 [9], replicated, may hold values from 1 to 8, 32 in all
- stats_left: float32 [8, 4, 2, 256, 256], P('dp', 'shard'), may hold values from -6 to 6
- stats_right: float32 [8, 4, 2, 256, 256], P('dp', 'shard'), may hold values from -6 to 6
- root_left: bfloat16 [8, 4, 2, 256, 256], P('dp', 'shard'), may hold values from -0.375 to 0.375
- root_right: bfloat16 [8, 4, 2, 256, 256], P('dp', 'shard'), may hold values from -0.375 to 0.375
- second_moment: float32 [8, 4, 2, 256, 256], P('dp', 'shard'), may hold values from 0.0015 to 0.6
- master: float32 [8, 4, 2, 256, 256], P('dp', 'shard'), may hold values from -6 to 6
Outputs:
- new_left: float32 [8, 4, 2, 256, 256], P('dp', 'shard')
- new_right: float32 [8, 4, 2, 256, 256], P('dp', 'shard')
- new_moment: float32 [8, 4, 2, 256, 256], P('dp', 'shard')
- new_master: float32 [8, 4, 2, 256, 256], P('dp', 'shard')
- regathered: bfloat16 [32, 256, 256], P('shard')
Inputs may be any that keep to these rules, and one draw needn't show every extreme that they name: `owners`: in each aligned block of 8 rows (one column) no dp index is named more than 2 times; some column names one exactly 2 times. `weight_blocks`: sums to 32; the largest is 8.
All inputs are finite; a program needn't handle non-finite values.
Results may differ from a plain program's by a relative error of at most 0.0047.
Values may be sent and summed in bfloat16 or wider, within the bound.
No kernel may reach another device: no remote copies, remote signals or barrier semaphores. Data moves between devices by JAX's collectives and lax.ppermute only.
A program may use at most 128 MiB of HBM per device.

v0:
```python
import jax
import jax.numpy as jnp
from jax import lax
from jax.sharding import PartitionSpec as P

BETA = 0.95
RATE = 0.3
ADAM_EPS = 1e-08
NORM_EPS = 1e-06


def local(
    grad_partials,
    owners,
    weight_blocks,
    stats_left,
    stats_right,
    root_left,
    root_right,
    second_moment,
    master,
):
    replica = lax.axis_index("dp")
    column = lax.axis_index("shard")
    replicas = lax.axis_size("dp")
    local_grads = grad_partials[0]
    column_blocks = local_grads.shape[0]
    slot_count = stats_left.shape[2]
    owner_of = owners[:, 0]
    onehot = (owner_of[:, None] == jnp.arange(replicas, dtype=jnp.int32)[None, :]).astype(jnp.int32)
    slot_rank = jnp.sum((jnp.cumsum(onehot, axis=0) - onehot) * onehot, axis=1)
    matches = (owner_of[None, None, :] == jnp.arange(replicas, dtype=jnp.int32)[:, None, None]) & (
        slot_rank[None, None, :] == jnp.arange(slot_count, dtype=jnp.int32)[None, :, None]
    )
    slot_table = jnp.sum(
        matches.astype(jnp.int32) * jnp.arange(column_blocks, dtype=jnp.int32)[None, None, :],
        axis=2,
    )
    slot_live = jnp.any(matches, axis=2)
    my_table = lax.dynamic_index_in_dim(slot_table, replica, 0, keepdims=False)
    my_live = lax.dynamic_index_in_dim(slot_live, replica, 0, keepdims=False)
    live_float = my_live.astype(jnp.float32)[:, None, None]
    summed = lax.psum(local_grads.astype(jnp.float32), "dp")
    owned_grad = jnp.take(summed, my_table, axis=0) * live_float
    left = stats_left[0, 0]
    right = stats_right[0, 0]
    moment = second_moment[0, 0]
    weights = master[0, 0]
    global_block = column * column_blocks + my_table
    ends = jnp.cumsum(weight_blocks)
    weight_id = jnp.sum((global_block[:, None] >= ends[None, :]).astype(jnp.int32), axis=1)
    member = (
        weight_id[:, None] == jnp.arange(weight_blocks.shape[0], dtype=jnp.int32)[None, :]
    ).astype(jnp.float32) * my_live.astype(jnp.float32)[:, None]
    vnew = BETA * moment + (1.0 - BETA) * owned_grad * owned_grad
    adam = owned_grad / (jnp.sqrt(vnew) + ADAM_EPS)
    adam_terms = jnp.sum(member * jnp.sum(adam * adam, axis=(1, 2))[:, None], axis=0)
    norm_adam = lax.psum(adam_terms, ("dp", "shard"))
    highest = lax.Precision.HIGHEST
    lnew = BETA * left + (1.0 - BETA) * jnp.einsum(
        "sij,skj->sik", owned_grad, owned_grad, precision=highest
    )
    rnew = BETA * right + (1.0 - BETA) * jnp.einsum(
        "sji,sjk->sik", owned_grad, owned_grad, precision=highest
    )
    grad_half = owned_grad.astype(jnp.bfloat16)
    inner = jnp.einsum(
        "sij,sjk->sik", root_left[0, 0], grad_half, preferred_element_type=jnp.float32
    ).astype(jnp.bfloat16)
    precond = jnp.einsum(
        "sij,sjk->sik", inner, root_right[0, 0], preferred_element_type=jnp.float32
    )
    prec_terms = jnp.sum(member * jnp.sum(precond * precond, axis=(1, 2))[:, None], axis=0)
    norm_prec = lax.psum(prec_terms, ("dp", "shard"))
    scales = jnp.sqrt(norm_adam / (norm_prec + NORM_EPS))
    slot_scale = jnp.sum(member * scales[None, :], axis=1)
    wnew = weights - RATE * slot_scale[:, None, None] * precond
    live_mask = my_live[:, None, None]
    out_left = jnp.where(live_mask, lnew, left)
    out_right = jnp.where(live_mask, rnew, right)
    out_moment = jnp.where(live_mask, vnew, moment)
    out_master = jnp.where(live_mask, wnew, weights)
    gathered = lax.all_gather(out_master.astype(jnp.bfloat16), "dp", axis=0, tiled=True)
    regathered = jnp.take(gathered, owner_of * slot_count + slot_rank, axis=0)
    return (
        out_left[None, None],
        out_right[None, None],
        out_moment[None, None],
        out_master[None, None],
        regathered,
    )


def solution(mesh):
    in_specs = (
        P("dp", "shard", None, None),
        P("shard", None),
        P(),
        P("dp", "shard", None, None, None),
        P("dp", "shard", None, None, None),
        P("dp", "shard", None, None, None),
        P("dp", "shard", None, None, None),
        P("dp", "shard", None, None, None),
        P("dp", "shard", None, None, None),
    )
    out_specs = (
        P("dp", "shard", None, None, None),
        P("dp", "shard", None, None, None),
        P("dp", "shard", None, None, None),
        P("dp", "shard", None, None, None),
        P("shard", None, None),
    )
    return jax.shard_map(local, mesh=mesh, in_specs=in_specs, out_specs=out_specs, check_vma=False)
```

profile of v0, /device:TPU:0, one launch (start us, length us, event | category | flops | bytes accessed | tf_op | source)
XLA Modules:
  0.0 161.0 jit_solution(1101177767100305149)
XLA Ops:
  7.2 0.0 copy-start
  7.2 0.0 all-reduce.3.cloned.1.call-start
  7.2 2.7 %bitcast_convert_fusion = f32[8,256,256]{2,1,0:T(8,128)} fusion(bf16[1,8,256,256]{3,2,1,0:T(8,128)(2,1)} %param.9), kind=kLoop, calls=%fused_computation.12 | loop fusion | flops 524288 | bytes 3145728 | tf_op jit(solution)/shard_map/convert_element_type | solution.py:43
  10.0 0.0 all-reduce.3.cloned.1.call-update
  10.0 0.0 copy-start.2
  10.0 0.0 all-gather.2.cloned.1.call-start
  10.1 0.1 iota_compare_fusion.1
  10.2 0.2 select_reduce_fusion
  10.4 0.1 and_reduce_fusion
  10.5 0.2 dynamic-slice_reduce_fusion
  10.7 0.1 fusion.34
  10.9 0.2 dynamic-slice_reduce_fusion.1
  11.1 0.2 reduce-window.8
  11.3 0.2 fusion.36
  11.5 66.6 %all-reduce.3.cloned.1.call-done = f32[8,256,256]{2,1,0:T(8,128)} async-done(((f32[8,256,256]{2,1,0:T(8,128)}), f32[8,256,256]{2,1,0:T(8,128)}) %all-reduce.3.cloned.1.call-update) | async-done | bytes 2097168 | tf_op jit(solution)/shard_map/psum | solution.py:43
  78.1 2.2 %gather_fusion = f32[2,256,256]{2,1,0:T(8,128)S(1)} fusion(f32[8,256,256]{2,1,0:T(8,128)} %all-reduce.3.cloned.1.call-done, s32[1024]{0:T(1024)S(1)} %pad_clamp_fusion.1), kind=kCustom, calls=%fused_computation | custom fusion | bytes 1048584 | tf_op jit(solution)/shard_map/jit(_take)/gather | solution.py:44
  80.2 0.0 copy-done.1
  80.2 0.5 fusion.15
  80.7 0.0 copy-done
  80.7 0.7 multiply_reduce_fusion
  81.4 0.1 multiply_reduce_fusion.2
  81.5 39.8 %all-reduce = (f32[9]{0:T(128)S(1)}, f32[9]{0:T(128)S(1)}) all-reduce(f32[9]{0:T(128)S(1)} %get-tuple-element.6, f32[9]{0:T(128)S(1)} %get-tuple-element.5), channel_id=1, replica_groups=mesh['dp'=8,'shard'=4] {'dp','shard'}, use_global_device_ids=true, to_apply=%region_9.10 | all-reduce | flops 18 | bytes 144 | tf_op jit(solution)/shard_map/psum | solution.py:58
  121.3 0.2 multiply_reduce_fusion.1
  121.5 0.0 copy-done.2
  121.5 1.0 fusion.43
  122.5 0.0 all-gather.2.cloned.1.call-update
  122.6 2.0 %fusion.2 = f32[1,1,2,256,256]{4,3,2,1,0:T(8,128)} fusion(f32[1,1,2,256,256]{4,3,2,1,0:T(8,128)S(1)} %copy-done.3, f32[2,256,256]{2,1,0:T(8,128)S(1)} %gather_fusion, f32[2]{0:T(128)S(1)} %convert_element_type.39, pred[2]{0:T(512)(128)(4,1)S(1)} %compare_and_fusion, pred[2]{0:T(512)(128)(4,1)S(1)} %dynamic-slice_reduce_fusion), kind=kOutput, calls=%fused_computation.5 | convolution fusion | flops 403439616 | bytes 1572876 | tf_op jit(solution)/shard_map/sji,sjk->sik/dot_general | solution.py:63
  124.6 1.7 %fusion.5 = f32[1,1,2,256,256]{4,3,2,1,0:T(8,128)} fusion(f32[1,1,2,256,256]{4,3,2,1,0:T(8,128)S(1)} %copy-done.4, f32[2,256,256]{2,1,0:T(8,128)S(1)} %gather_fusion, f32[2]{0:T(128)S(1)} %convert_element_type.39, pred[2]{0:T(512)(128)(4,1)S(1)} %compare_and_fusion, pred[2]{0:T(512)(128)(4,1)S(1)} %dynamic-slice_reduce_fusion), kind=kOutput, calls=%fused_computation.9 | convolution fusion | flops 403439616 | bytes 1572876 | tf_op jit(solution)/shard_map/sij,skj->sik/dot_general | solution.py:60
  126.2 1.0 fusion.8
  127.2 23.6 %all-gather.2.cloned.1.call-done = bf16[16,256,256]{2,1,0:T(8,128)(2,1)} async-done(((bf16[2,256,256]{2,1,0:T(8,128)(2,1)}), bf16[16,256,256]{2,1,0:T(8,128)(2,1)}) %all-gather.2.cloned.1.call-update) | async-done | bytes 2097168 | tf_op jit(solution)/shard_map/all_gather | solution.py:83
  150.9 2.2 %gather_fusion.1 = bf16[8,256,256]{2,1,0:T(8,128)(2,1)S(1)} fusion(bf16[16,256,256]{2,1,0:T(8,128)(2,1)} %all-gather.2.cloned.1.call-done, s32[1024]{0:T(1024)S(1)} %pad_clamp_fusion), kind=kCustom, calls=%fused_computation.1 | custom fusion | bytes 2097184 | tf_op jit(solution)/shard_map/jit(_take)/gather | solution.py:84
  153.1 1.1 broadcast_select_fusion
  (22 shorter events, 0.1 us)
Async XLA Ops:
  7.2 73.6 %copy-start = (bf16[1,1,2,256,256]{4,3,2,1,0:T(8,128)(2,1)S(1)}, bf16[1,1,2,256,256]{4,3,2,1,0:T(8,128)(2,1)}, u32[]{:S(2)}) copy-start(bf16[1,1,2,256,256]{4,3,2,1,0:T(8,128)(2,1)} %param.15) | copy-start | bytes 786436
  7.2 2.9 %copy-start.6 = (s32[8,1]{0,1:T(1,128)S(1)}, s32[8,1]{0,1:T(1,128)}, u32[]{:S(2)}) copy-start(s32[8,1]{0,1:T(1,128)} %param.10) | copy-start | bytes 100
  7.2 3.9 %copy-start.7 = (s32[9]{0:T(128)S(1)}, s32[9]{0:T(128)}, u32[]{:S(2)}) copy-start(s32[9]{0:T(128)} %param.11) | copy-start | bytes 112
  7.2 70.9 %all-reduce.3.cloned.1.call-start = ((), (), s32[]{:S(2)}) async-start(), calls=%async_computation | async-start | bytes 4194304 | tf_op jit(solution)/shard_map/psum | solution.py:43
  10.0 70.2 %copy-start.1 = (f32[1,1,2,256,256]{4,3,2,1,0:T(8,128)S(1)}, f32[1,1,2,256,256]{4,3,2,1,0:T(8,128)}, u32[]{:S(2)}) copy-start(f32[1,1,2,256,256]{4,3,2,1,0:T(8,128)} %param.16) | copy-start | bytes 1572868
  10.0 70.7 %copy-start.5 = (bf16[1,1,2,256,256]{4,3,2,1,0:T(8,128)(2,1)S(1)}, bf16[1,1,2,256,256]{4,3,2,1,0:T(8,128)(2,1)}, u32[]{:S(2)}) copy-start(bf16[1,1,2,256,256]{4,3,2,1,0:T(8,128)(2,1)} %param.14) | copy-start | bytes 786436
  10.0 111.5 %copy-start.2 = (f32[1,1,2,256,256]{4,3,2,1,0:T(8,128)S(1)}, f32[1,1,2,256,256]{4,3,2,1,0:T(8,128)}, u32[]{:S(2)}) copy-start(f32[1,1,2,256,256]{4,3,2,1,0:T(8,128)} %param.17) | copy-start | bytes 1572868
  10.0 140.8 %all-gather.2.cloned.1.call-start = ((), (), s32[]{:S(2)}) async-start(), calls=%async_computation.1 | async-start | bytes 2359296 | tf_op jit(solution)/shard_map/all_gather | solution.py:83
  80.7 41.9 %copy-start.3 = (f32[1,1,2,256,256]{4,3,2,1,0:T(8,128)S(1)}, f32[1,1,2,256,256]{4,3,2,1,0:T(8,128)}, u32[]{:S(2)}) copy-start(f32[1,1,2,256,256]{4,3,2,1,0:T(8,128)} %param.13) | copy-start | bytes 1572868
  81.4 43.2 %copy-start.4 = (f32[1,1,2,256,256]{4,3,2,1,0:T(8,128)S(1)}, f32[1,1,2,256,256]{4,3,2,1,0:T(8,128)}, u32[]{:S(2)}) copy-start(f32[1,1,2,256,256]{4,3,2,1,0:T(8,128)} %param.12) | copy-start | bytes 1572868
Sparse Core Ops, SparseCore 0:
  10.4 67.6 all-reduce.2
  122.7 28.1 all-gather.1
where the time goes:
time: 161 us
  waiting for transfers between devices  90.2 us (56%)
  blocking collectives  39.8 us (25%)
  between operations  14.2 us (9%)
  other arithmetic  7.65 us (5%)
  local copies, waits for them, and re-layouts  4.78 us (3%)
  matrix products  4.3 us (3%)
    psum x1, waiting for transfers between devices, local(): summed = lax.psum(local_grads.astype(jnp.float32), 'dp')  66.6 us
    psum x1, blocking collectives, local(): norm_adam = lax.psum(adam_terms, ('dp', 'shard'))  39.8 us
    all_gather x1, waiting for transfers between devices, local(): lax.all_gather(out_master.astype(jnp.bfloat16), 'dp', axis=0, tiled=True)  23.6 us
  transfers between devices with their start and end apart: 2, of which 2 were waited for; matrix products, arithmetic and copies ran while one was open for 4% of the time, Pallas kernels for 0%

commit v1 on v0

--- a/solution.py
+++ b/solution.py
@@ -2,6 +2,7 @@
 import jax.numpy as jnp
 from jax import lax
 from jax.sharding import PartitionSpec as P
+from jax.lax import psum
 
 BETA = 0.95
 RATE = 0.3
@@ -55,7 +56,7 @@
     vnew = BETA * moment + (1.0 - BETA) * owned_grad * owned_grad
     adam = owned_grad / (jnp.sqrt(vnew) + ADAM_EPS)
     adam_terms = jnp.sum(member * jnp.sum(adam * adam, axis=(1, 2))[:, None], axis=0)
-    norm_adam = lax.psum(adam_terms, ("dp", "shard"))
+    norm_adam = psum(psum(adam_terms, "shard"), axis_name="dp")
     highest = lax.Precision.HIGHEST
     lnew = BETA * left + (1.0 - BETA) * jnp.einsum(
         "sij,skj->sik", owned_grad, owned_grad, precision=highest

time: 161 us -> 183 us (1.14)
  blocking collectives: 39.8 us -> 60.4 us
    psum x1 -> x3, blocking collectives: 39.8 us -> 60.4 us  [the longest x1 36.9 us: local(): norm_prec = lax.psum(prec_terms, ('dp', 'shard'))]
  transfers between devices with their start and end apart: 2 -> 2, of which waited for: 2 -> 2; matrix products, arithmetic and copies ran while one was open for 4% -> 3% of each run, Pallas kernels for 0% -> 0%
where the time goes in v1:
time: 183 us
  waiting for transfers between devices  91.7 us (50%)
  blocking collectives  60.4 us (33%)
  between operations  14.2 us (8%)
  other arithmetic  7.65 us (4%)
  local copies, waits for them, and re-layouts  4.78 us (3%)
  matrix products  4.3 us (2%)
    psum x1, waiting for transfers between devices, local(): summed = lax.psum(local_grads.astype(jnp.float32), 'dp')  66.6 us
    psum x1, blocking collectives, local(): norm_prec = lax.psum(prec_terms, ('dp', 'shard'))  36.9 us
    all_gather x1, waiting for transfers between devices, local(): lax.all_gather(out_master.astype(jnp.bfloat16), 'dp', axis=0, tiled=True)  25.1 us
    psum x2, blocking collectives, local(): norm_adam = psum(psum(adam_terms, 'shard'), axis_name='dp')  23.5 us
  transfers between devices with their start and end apart: 2, of which 2 were waited for; matrix products, arithmetic and copies ran while one was open for 3% of the time, Pallas kernels for 0%

profile of v1, /device:TPU:0, one launch (start us, length us, event | category | flops | bytes accessed | tf_op | source)
XLA Modules:
  0.0 183.1 jit_solution(7444548938891755676)
XLA Ops:
  7.2 0.0 copy-start
  7.2 0.0 all-reduce.2.cloned.1.call-start
  7.2 2.7 %bitcast_convert_fusion = f32[8,256,256]{2,1,0:T(8,128)} fusion(bf16[1,8,256,256]{3,2,1,0:T(8,128)(2,1)} %param.9), kind=kLoop, calls=%fused_computation.12 | loop fusion | flops 524288 | bytes 3145728 | tf_op jit(solution)/shard_map/convert_element_type | solution.py:44
  10.0 0.0 all-reduce.2.cloned.1.call-update
  10.0 0.0 copy-start.2
  10.0 0.0 all-gather.2.cloned.1.call-start
  10.1 0.1 iota_compare_fusion.1
  10.2 0.2 select_reduce_fusion
  10.4 0.1 and_reduce_fusion
  10.5 0.2 dynamic-slice_reduce_fusion
  10.7 0.1 fusion.34
  10.9 0.2 dynamic-slice_reduce_fusion.1
  11.1 0.2 reduce-window.8
  11.3 0.2 fusion.36
  11.5 66.6 %all-reduce.2.cloned.1.call-done = f32[8,256,256]{2,1,0:T(8,128)} async-done(((f32[8,256,256]{2,1,0:T(8,128)}), f32[8,256,256]{2,1,0:T(8,128)}) %all-reduce.2.cloned.1.call-update) | async-done | bytes 2097168 | tf_op jit(solution)/shard_map/psum | solution.py:44
  78.1 2.2 %gather_fusion = f32[2,256,256]{2,1,0:T(8,128)S(1)} fusion(f32[8,256,256]{2,1,0:T(8,128)} %all-reduce.2.cloned.1.call-done, s32[1024]{0:T(1024)S(1)} %pad_clamp_fusion.1), kind=kCustom, calls=%fused_computation | custom fusion | bytes 1048584 | tf_op jit(solution)/shard_map/jit(_take)/gather | solution.py:45
  80.2 0.0 copy-done.1
  80.2 0.5 fusion.15
  80.7 0.7 multiply_reduce_fusion
  81.4 0.1 multiply_reduce_fusion.2
  81.5 10.0 %psum.29 = f32[9]{0:T(128)S(1)} all-reduce(f32[9]{0:T(128)S(1)} %get-tuple-element.6), channel_id=1, replica_groups=mesh['dp'=8,'shard'=4] {'shard'}, use_global_device_ids=true, to_apply=%region_9.10 | all-reduce | flops 9 | bytes 72 | tf_op jit(solution)/shard_map/psum | solution.py:59
  91.5 13.6 %psum.30 = f32[9]{0:T(128)S(1)} all-reduce(f32[9]{0:T(128)S(1)} %psum.29), channel_id=1, replica_groups=mesh['dp'=8,'shard'=4] {'dp'}, use_global_device_ids=true, to_apply=%region_10.11 | all-reduce | flops 9 | bytes 72 | tf_op jit(solution)/shard_map/psum | solution.py:59
  105.0 36.9 %psum.31 = f32[9]{0:T(128)S(1)} all-reduce(f32[9]{0:T(128)S(1)} %get-tuple-element.5), channel_id=1, replica_groups=mesh['dp'=8,'shard'=4] {'dp','shard'}, use_global_device_ids=true, to_apply=%region_13.14 | all-reduce | flops 9 | bytes 72 | tf_op jit(solution)/shard_map/psum | solution.py:75
  141.9 0.2 multiply_reduce_fusion.1
  142.1 1.0 fusion.43
  143.2 0.0 all-gather.2.cloned.1.call-update
  143.2 2.0 %fusion.2 = f32[1,1,2,256,256]{4,3,2,1,0:T(8,128)} fusion(f32[1,1,2,256,256]{4,3,2,1,0:T(8,128)S(1)} %copy-done.3, f32[2,256,256]{2,1,0:T(8,128)S(1)} %gather_fusion, f32[2]{0:T(128)S(1)} %convert_element_type.39, pred[2]{0:T(512)(128)(4,1)S(1)} %compare_and_fusion, pred[2]{0:T(512)(128)(4,1)S(1)} %dynamic-slice_reduce_fusion), kind=kOutput, calls=%fused_computation.5 | convolution fusion | flops 403439616 | bytes 1572876 | tf_op jit(solution)/shard_map/sji,sjk->sik/dot_general | solution.py:64
  145.2 1.7 fusion.5
  146.9 1.0 fusion.8
  147.8 25.1 %all-gather.2.cloned.1.call-done = bf16[16,256,256]{2,1,0:T(8,128)(2,1)} async-done(((bf16[2,256,256]{2,1,0:T(8,128)(2,1)}), bf16[16,256,256]{2,1,0:T(8,128)(2,1)}) %all-gather.2.cloned.1.call-update) | async-done | bytes 2097168 | tf_op jit(solution)/shard_map/all_gather | solution.py:84
  172.9 2.2 %gather_fusion.1 = bf16[8,256,256]{2,1,0:T(8,128)(2,1)S(1)} fusion(bf16[16,256,256]{2,1,0:T(8,128)(2,1)} %all-gather.2.cloned.1.call-done, s32[1024]{0:T(1024)S(1)} %pad_clamp_fusion), kind=kCustom, calls=%fused_computation.1 | custom fusion | bytes 2097184 | tf_op jit(solution)/shard_map/jit(_take)/gather | solution.py:85
  175.1 1.1 broadcast_select_fusion
  (24 shorter events, 0.1 us)
Async XLA Ops:
  7.2 73.6 %copy-start = (bf16[1,1,2,256,256]{4,3,2,1,0:T(8,128)(2,1)S(1)}, bf16[1,1,2,256,256]{4,3,2,1,0:T(8,128)(2,1)}, u32[]{:S(2)}) copy-start(bf16[1,1,2,256,256]{4,3,2,1,0:T(8,128)(2,1)} %param.15) | copy-start | bytes 786436
  7.2 2.9 %copy-start.6 = (s32[8,1]{0,1:T(1,128)S(1)}, s32[8,1]{0,1:T(1,128)}, u32[]{:S(2)}) copy-start(s32[8,1]{0,1:T(1,128)} %param.10) | copy-start | bytes 100
  7.2 3.9 %copy-start.7 = (s32[9]{0:T(128)S(1)}, s32[9]{0:T(128)}, u32[]{:S(2)}) copy-start(s32[9]{0:T(128)} %param.11) | copy-start | bytes 112
  7.2 70.9 %all-reduce.2.cloned.1.call-start = ((), (), s32[]{:S(2)}) async-start(), calls=%async_computation | async-start | bytes 4194304 | tf_op jit(solution)/shard_map/psum | solution.py:44
  10.0 70.2 %copy-start.1 = (f32[1,1,2,256,256]{4,3,2,1,0:T(8,128)S(1)}, f32[1,1,2,256,256]{4,3,2,1,0:T(8,128)}, u32[]{:S(2)}) copy-start(f32[1,1,2,256,256]{4,3,2,1,0:T(8,128)} %param.16) | copy-start | bytes 1572868
  10.0 70.7 %copy-start.5 = (bf16[1,1,2,256,256]{4,3,2,1,0:T(8,128)(2,1)S(1)}, bf16[1,1,2,256,256]{4,3,2,1,0:T(8,128)(2,1)}, u32[]{:S(2)}) copy-start(bf16[1,1,2,256,256]{4,3,2,1,0:T(8,128)(2,1)} %param.14) | copy-start | bytes 786436
  10.0 132.1 %copy-start.2 = (f32[1,1,2,256,256]{4,3,2,1,0:T(8,128)S(1)}, f32[1,1,2,256,256]{4,3,2,1,0:T(8,128)}, u32[]{:S(2)}) copy-start(f32[1,1,2,256,256]{4,3,2,1,0:T(8,128)} %param.17) | copy-start | bytes 1572868
  10.0 162.9 %all-gather.2.cloned.1.call-start = ((), (), s32[]{:S(2)}) async-start(), calls=%async_computation.1 | async-start | bytes 2359296 | tf_op jit(solution)/shard_map/all_gather | solution.py:84
  80.7 62.5 %copy-start.3 = (f32[1,1,2,256,256]{4,3,2,1,0:T(8,128)S(1)}, f32[1,1,2,256,256]{4,3,2,1,0:T(8,128)}, u32[]{:S(2)}) copy-start(f32[1,1,2,256,256]{4,3,2,1,0:T(8,128)} %param.13) | copy-start | bytes 1572868
  81.4 63.8 %copy-start.4 = (f32[1,1,2,256,256]{4,3,2,1,0:T(8,128)S(1)}, f32[1,1,2,256,256]{4,3,2,1,0:T(8,128)}, u32[]{:S(2)}) copy-start(f32[1,1,2,256,256]{4,3,2,1,0:T(8,128)} %param.12) | copy-start | bytes 1572868
Sparse Core Ops, SparseCore 0:
  10.4 67.6 all-reduce.1
  143.3 29.5 all-gather.1
